TPU v7x, 256 devices: a whole 4x4x8 slice. The times are simulated.
256 devices in a mesh: seq: 64 (over z_hi, x, y, core), tp: 4 (over z_lo).
Axes of the slice: x: 4, y: 4, z: 8 (z_hi: 2, z_lo: 4; z = z_hi * 4 + z_lo), core: 2. Of those that a mesh axis runs over, the one named last changes fastest.
Arguments:
- query_rows: bfloat16 [16384, 4096], P('seq', 'tp'), may hold values from -6 to 6
- key_rows: bfloat16 [16384, 4096], P('seq', 'tp'), may hold values from -6 to 6
- value_rows: bfloat16 [16384, 4096], P('seq', 'tp'), may hold values from -6 to 6
- short_filter: float32 [3, 3, 4096], P(None, None, 'tp'), may hold values from -3 to 3
- long_filter: bfloat16 [16384, 4096], P('seq', 'tp'), may hold values from -1.1 to 1.1, as said below
- skip_gain: float32 [4096], P('tp'), may hold values from -4 to 4
- out_weight: bfloat16 [4096, 4096], P('seq', 'tp'), may hold values from -0.09375 to 0.09375
Outputs:
- projected: bfloat16 [16384, 4096], P('seq', 'tp')
Inputs may be any that keep to these rules, and one draw needn't show every extreme that they name: `long_filter`: taps of the long filter.
All inputs are finite; a program needn't handle non-finite values.
Results may differ from a plain program's by a relative error of at most 0.0061.
Values may be sent and summed in bfloat16 or wider, within the bound.
No kernel may reach another device: no remote copies, remote signals or barrier semaphores. Data moves between devices by JAX's collectives and lax.ppermute only.
A program may use at most 64 MiB of HBM per device.

v0:
```python
import math
import numpy as np
import jax
import jax.numpy as jnp
from jax import lax
from jax.sharding import PartitionSpec as P

TRANSFORM_PRECISION = lax.Precision.HIGH


def shifted(value, axis, by):
    size = lax.axis_size(axis)
    pairs = [(i, i + by) for i in range(size) if 0 <= i + by < size]
    return lax.ppermute(value, axis, pairs)


def make_tables(blocks, tokens):
    outer = 2 * blocks
    period = outer * tokens
    k1 = np.arange(outer, dtype=np.int64)
    n1 = np.arange(blocks, dtype=np.int64)
    n2 = np.arange(tokens, dtype=np.int64)
    first = 2.0 * np.pi * (k1[:, None] * n1[None, :] % outer) / outer
    first_table = np.concatenate([np.cos(first), -np.sin(first)], 0)
    twist = 2.0 * np.pi * (k1[:, None] * n2[None, :] % period) / period
    twist_cos = np.cos(twist)[:, None, :]
    twist_sin = np.sin(twist)[:, None, :]
    inner = 2.0 * np.pi * (n2[:, None] * n2[None, :] % tokens) / tokens
    b_cos = np.cos(inner)
    b_sin = np.sin(inner)
    forward = np.block([[b_cos, -b_sin], [b_sin, b_cos]])
    backward = np.block([[b_cos, b_sin], [-b_sin, b_cos]])
    last = 2.0 * np.pi * (n1[:, None] * k1[None, :] % outer) / outer
    last_table = np.concatenate([np.cos(last), -np.sin(last)], 1) / period
    as32 = lambda a: jnp.asarray(a, jnp.float32)
    return tuple(
        (as32(a) for a in (first_table, twist_cos, twist_sin, forward, backward, last_table))
    )


def dot(a, b):
    return jnp.dot(a, b, precision=TRANSFORM_PRECISION, preferred_element_type=jnp.float32)


def long_conv(pieces, per_device, tables):
    first_table, twist_cos, twist_sin, forward, backward, last_table = tables
    blocks, both, tokens = pieces.shape
    outer = 2 * blocks
    spec = dot(first_table, pieces.reshape(blocks, both * tokens)).reshape(2, outer, both, tokens)
    s_real, s_imag = (spec[0], spec[1])
    w_real = s_real * twist_cos + s_imag * twist_sin
    w_imag = s_imag * twist_cos - s_real * twist_sin
    twisted = jnp.concatenate([w_real, w_imag], -1).reshape(outer * both, 2 * tokens)
    u = dot(twisted, forward).reshape(outer, both, 2 * tokens)
    u_real, u_imag = (u[:, :per_device, :tokens], u[:, :per_device, tokens:])
    f_real, f_imag = (u[:, per_device:, :tokens], u[:, per_device:, tokens:])
    p_real = u_real * f_real - u_imag * f_imag
    p_imag = u_real * f_imag + u_imag * f_real
    product = jnp.concatenate([p_real, p_imag], -1).reshape(outer * per_device, 2 * tokens)
    q = dot(product, backward).reshape(outer, per_device, 2 * tokens)
    q_real, q_imag = (q[..., :tokens], q[..., tokens:])
    r_real = q_real * twist_cos - q_imag * twist_sin
    r_imag = q_real * twist_sin + q_imag * twist_cos
    stacked = jnp.stack([r_real, r_imag], 0).reshape(2 * outer, per_device * tokens)
    result = dot(last_table, stacked)
    return result.reshape(blocks, per_device, tokens).astype(jnp.bfloat16)


def causal_short(rows, tail, taps):
    extended = jnp.concatenate([tail, rows], 0)
    return (
        taps[0] * extended[2:].astype(jnp.float32)
        + taps[1] * extended[1:-1].astype(jnp.float32)
        + taps[2] * extended[:-2].astype(jnp.float32)
    )


def body(query_rows, key_rows, value_rows, short_filter, long_filter, skip_gain, out_weight):
    tokens_here, channels = query_rows.shape
    groups = lax.axis_size("seq")
    per_device = channels // groups
    tables = make_tables(groups, tokens_here)
    tails = shifted((query_rows[-2:], key_rows[-2:], value_rows[-2:]), "seq", 1)
    query_mix = causal_short(query_rows, tails[0], short_filter[:, 0, :])
    key_mix = causal_short(key_rows, tails[1], short_filter[:, 1, :])
    value_mix = causal_short(value_rows, tails[2], short_filter[:, 2, :])
    gated = (key_mix * value_mix).astype(jnp.bfloat16)
    gated_cols = gated.T.reshape(groups, per_device, tokens_here)
    filter_cols = long_filter.T.reshape(groups, per_device, tokens_here)
    outgoing = jnp.concatenate([gated_cols, filter_cols], 1)
    pieces = lax.all_to_all(outgoing, "seq", split_axis=0, concat_axis=0, tiled=True)
    mixed = long_conv(pieces, per_device, tables)
    returned = lax.all_to_all(mixed, "seq", split_axis=0, concat_axis=0, tiled=True)
    conv = returned.reshape(channels, tokens_here).T
    inner = (query_mix * (conv.astype(jnp.float32) + skip_gain * gated.astype(jnp.float32))).astype(
        jnp.bfloat16
    )
    weights = lax.all_gather(out_weight, "seq", axis=0, tiled=True)
    total = jnp.dot(
        lax.all_gather(inner, "tp", axis=1, tiled=True), weights, preferred_element_type=jnp.float32
    )
    return total.astype(jnp.bfloat16)


def solution(mesh):
    placed = (
        P("seq", "tp"),
        P("seq", "tp"),
        P("seq", "tp"),
        P(None, None, "tp"),
        P("seq", "tp"),
        P("tp"),
        P("seq", "tp"),
    )
    return jax.shard_map(
        body, mesh=mesh, in_specs=placed, out_specs=P("seq", "tp"), check_vma=False
    )
```

profile of v0, /device:TPU:1, one launch (start us, length us, event | category | flops | bytes accessed | tf_op | source)
XLA Modules:
  0.0 303.2 jit_solution(137879276982766816)
XLA Ops:
  7.5 4.6 %collective-permute-start.1 = (bf16[2,1024]{0,1:T(8,128)(2,1)S(1)}, bf16[2,1024]{0,1:T(8,128)(2,1)S(1)}, u32[]{:S(2)}, u32[]{:S(2)}) collective-permute-start(bf16[2,1024]{0,1:T(8,128)(2,1)S(1)} %copy.23), channel_id=1, source_target_pairs={{0,4},{4,8},{8,12},{12,16},{16,20},{20,24},{24,28},{28,32},{32,36}... | collective-permute-start | bytes 12296 | tf_op jit(solution)/shard_map/ppermute | solution.py:14
  13.0 1.9 collective-permute-start.2
  14.9 0.9 fusion.19
  15.8 1.2 copy.22
  17.1 1.2 copy.25
  18.3 1.2 copy.28
  19.6 1.9 multiply_convert_fusion
  21.6 38.1 %all_to_all.10 = bf16[64,32,256]{2,1,0:T(8,128)(2,1)S(1)} all-to-all(bf16[64,32,256]{2,1,0:T(8,128)(2,1)S(1)} %pad_maximum_fusion.1), channel_id=1, replica_groups=mesh['seq'=64,'tp'=4] {'seq'}, dimensions={0} | all-to-all | bytes 2097152 | tf_op jit(solution)/shard_map/all_to_all | solution.py:91
  60.4 2.3 fusion.20
  63.7 1.2 fusion.4
  64.9 7.0 %fusion = f32[128,32,512]{2,0,1:T(8,128)S(1)} fusion(f32[512,512,1]{1,0,2:T(8,128)S(1)} %copy-done.1, f32[128,32,256]{2,0,1:T(8,128)S(1)} %get-tuple-element.6, f32[128,32,256]{2,0,1:T(8,128)S(1)} %get-tuple-element.5), kind=kOutput, calls=%fused_computation | convolution fusion | flops 6444548096 | bytes 17825792 | tf_op jit(solution)/shard_map/dot_general | solution.py:42
  73.2 3.5 %fusion.6 = f32[128,16,512]{2,0,1:T(8,128)S(1)} fusion(f32[512,512,1]{1,0,2:T(8,128)S(1)} %copy-done, f32[128,16,256]{2,0,1:T(8,128)S(1)} %get-tuple-element.8, f32[128,16,256]{2,0,1:T(8,128)S(1)} %get-tuple-element.7), kind=kOutput, calls=%fused_computation.11 | convolution fusion | flops 3222274048 | bytes 9437184 | tf_op jit(solution)/shard_map/dot_general | solution.py:42
  77.7 2.4 copy.33
  80.2 3.8 %copy.37 = f32[32,8,16,256]{3,1,2,0:T(8,128)S(1)} copy(f32[32,8,16,256]{3,2,1,0:T(8,128)S(1)} %bitcast.65) | data formatting | bytes 8388608
  84.0 1.4 convolution_convert_fusion
  85.4 1.2 copy.38
  86.5 15.5 %all-to-all-start.1 = ((bf16[64,16,256]{2,1,0:T(8,128)(2,1)}), bf16[64,16,256]{2,1,0:T(8,128)(2,1)S(1)}, u32[]{:S(2)}, u32[]{:S(2)}) async-start(bf16[64,16,256]{2,1,0:T(8,128)(2,1)} %bitcast.33), calls=%async_computation.1 | async-start | bytes 1048576 | tf_op jit(solution)/shard_map/all_to_all | solution.py:93
  102.3 3.5 %collective-permute-start = (bf16[2,1024]{0,1:T(8,128)(2,1)S(1)}, bf16[2,1024]{0,1:T(8,128)(2,1)S(1)}, u32[]{:S(2)}, u32[]{:S(2)}) collective-permute-start(bf16[2,1024]{0,1:T(8,128)(2,1)S(1)} %copy.20), channel_id=1, source_target_pairs={{0,4},{4,8},{8,12},{12,16},{16,20},{20,24},{24,28},{28,32},{32,36}... | collective-permute-start | bytes 12296 | tf_op jit(solution)/shard_map/ppermute | solution.py:14
  106.0 4.8 %collective-permute-done = bf16[2,1024]{0,1:T(8,128)(2,1)S(1)} collective-permute-done((bf16[2,1024]{0,1:T(8,128)(2,1)S(1)}, bf16[2,1024]{0,1:T(8,128)(2,1)S(1)}, u32[]{:S(2)}, u32[]{:S(2)}) %collective-permute-start) | collective-permute-done | bytes 4128 | tf_op jit(solution)/shard_map/ppermute | solution.py:14
  110.8 11.9 %all-to-all-done.1 = bf16[64,16,256]{2,1,0:T(8,128)(2,1)S(1)} async-done(((bf16[64,16,256]{2,1,0:T(8,128)(2,1)}), bf16[64,16,256]{2,1,0:T(8,128)(2,1)S(1)}, u32[]{:S(2)}, u32[]{:S(2)}) %all-to-all-start.1) | async-done | bytes 524320 | tf_op jit(solution)/shard_map/all_to_all | solution.py:93
  122.7 1.9 fusion.12
  125.4 47.1 %all-gather.3.cloned.1.call-done = bf16[256,4096]{0,1:T(8,128)(2,1)} async-done(((bf16[256,1024]{0,1:T(8,128)(2,1)}), bf16[256,4096]{0,1:T(8,128)(2,1)}) %all-gather.3.cloned.1.call-update) | async-done | bytes 2097168 | tf_op jit(solution)/shard_map/all_gather | solution.py:100
  172.5 116.6 %all-gather.5.cloned.1.call-done = bf16[4096,1024]{1,0:T(8,128)(2,1)} async-done(((bf16[64,1024]{1,0:T(8,128)(2,1)}), bf16[4096,1024]{1,0:T(8,128)(2,1)}) %all-gather.5.cloned.1.call-update) | async-done | bytes 8388624 | tf_op jit(solution)/shard_map/all_gather | solution.py:98
  289.1 7.2 %convolution_convert_fusion.1 = bf16[256,1024]{1,0:T(8,128)(2,1)} fusion(bf16[256,4096]{0,1:T(8,128)(2,1)} %all-gather.3.cloned.1.call-done, bf16[4096,1024]{1,0:T(8,128)(2,1)} %all-gather.5.cloned.1.call-done), kind=kOutput, calls=%fused_computation.20 | convolution fusion | flops 2147745792 | bytes 11010048 | tf_op jit(solution)/shard_map/dot_general | solution.py:99
  (35 shorter events, 7.0 us)
Async XLA Ops:
  7.5 12.1 %collective-permute-start.1 = (bf16[2,1024]{0,1:T(8,128)(2,1)S(1)}, bf16[2,1024]{0,1:T(8,128)(2,1)S(1)}, u32[]{:S(2)}, u32[]{:S(2)}) collective-permute-start(bf16[2,1024]{0,1:T(8,128)(2,1)S(1)} %copy.23), channel_id=1, source_target_pairs={{0,4},{4,8},{8,12},{12,16},{16,20},{20,24},{24,28},{28,32},{32,36}... | collective-permute-start | bytes 12296 | tf_op jit(solution)/shard_map/ppermute | solution.py:14
  13.0 6.6 %collective-permute-start.2 = (bf16[2,1024]{0,1:T(8,128)(2,1)S(1)}, bf16[2,1024]{0,1:T(8,128)(2,1)S(1)}, u32[]{:S(2)}, u32[]{:S(2)}) collective-permute-start(bf16[2,1024]{0,1:T(8,128)(2,1)S(1)} %copy.26), channel_id=1, source_target_pairs={{0,4},{4,8},{8,12},{12,16},{16,20},{20,24},{24,28},{28,32},{32,36}... | collective-permute-start | bytes 12296 | tf_op jit(solution)/shard_map/ppermute | solution.py:14
  19.6 40.8 %copy-start.5 = (f32[256,64]{1,0:T(8,128)S(1)}, f32[256,64]{1,0:T(8,128)}, u32[]{:S(2)}) copy-start(f32[256,64]{1,0:T(8,128)} %constant.12.clone) | copy-start | bytes 196612
  62.7 0.9 copy-start.3
  62.7 1.0 copy-start.4
  63.7 1.3 copy-start.1
  72.0 1.2 copy-start
  80.2 3.8 %copy-start.6 = (f32[64,256]{1,0:T(8,128)S(1)}, f32[64,256]{1,0:T(8,128)}, u32[]{:S(2)}) copy-start(f32[64,256]{1,0:T(8,128)} %constant.17.clone) | copy-start | bytes 196612
  84.0 18.1 %copy-start.2 = (bf16[256,1024]{1,0:T(8,128)(2,1)S(1)}, bf16[256,1024]{1,0:T(8,128)(2,1)}, u32[]{:S(2)}) copy-start(bf16[256,1024]{1,0:T(8,128)(2,1)} %param.13) | copy-start | bytes 1572868
  84.0 38.7 %copy-start.7 = (f32[1024]{0:T(1024)S(1)}, f32[1024]{0:T(1024)}, u32[]{:S(2)}) copy-start(f32[1024]{0:T(1024)} %param.18) | copy-start | bytes 12292
  86.5 36.2 %all-to-all-start.1 = ((bf16[64,16,256]{2,1,0:T(8,128)(2,1)}), bf16[64,16,256]{2,1,0:T(8,128)(2,1)S(1)}, u32[]{:S(2)}, u32[]{:S(2)}) async-start(bf16[64,16,256]{2,1,0:T(8,128)(2,1)} %bitcast.33), calls=%async_computation.1 | async-start | bytes 1048576 | tf_op jit(solution)/shard_map/all_to_all | solution.py:93
  102.0 70.5 %all-gather.3.cloned.1.call-start = ((), (), s32[]{:S(2)}) async-start(), calls=%async_computation.2 | async-start | bytes 2621440 | tf_op jit(solution)/shard_map/all_gather | solution.py:100
  102.3 8.5 %collective-permute-start = (bf16[2,1024]{0,1:T(8,128)(2,1)S(1)}, bf16[2,1024]{0,1:T(8,128)(2,1)S(1)}, u32[]{:S(2)}, u32[]{:S(2)}) collective-permute-start(bf16[2,1024]{0,1:T(8,128)(2,1)S(1)} %copy.20), channel_id=1, source_target_pairs={{0,4},{4,8},{8,12},{12,16},{16,20},{20,24},{24,28},{28,32},{32,36}... | collective-permute-start | bytes 12296 | tf_op jit(solution)/shard_map/ppermute | solution.py:14
  124.6 164.5 %all-gather.5.cloned.1.call-start = ((), (), s32[]{:S(2)}) async-start(), calls=%async_computation.3 | async-start | bytes 8519680 | tf_op jit(solution)/shard_map/all_gather | solution.py:98
Sparse Core Ops, SparseCore 0:
  124.8 47.7 all-gather.2
  176.1 112.9 all-gather.4
where the time goes:
time: 304 us; the launch traced here: 303 us
  waiting for transfers between devices  181 us (60%)
  blocking collectives  38.1 us (13%)
  starting transfers between devices  25.6 us (8%)
  matrix products  21.4 us (7%)
  local copies, waits for them, and re-layouts  16.3 us (5%)
  between operations  13.7 us (5%)
  other arithmetic  6.97 us (2%)
    all_gather x1, waiting for transfers between devices, body(): weights = lax.all_gather(out_weight, 'seq', axis=0, tiled=True)  117 us
    all_gather x1, waiting for transfers between devices, body(): lax.all_gather(inner, 'tp', axis=1, tiled=True)  47.1 us
    all_to_all x1, blocking collectives, body(): lax.all_to_all(outgoing, 'seq', split_axis=0, concat_axis=0, tiled=True)  38.1 us
    all_to_all x1, starting transfers between devices, body(): lax.all_to_all(mixed, 'seq', split_axis=0, concat_axis=0, tiled=True)  15.5 us
    dot_general x4, matrix products, dot(): jnp.dot(a, b, precision=TRANSFORM_PRECISION, preferred_element_type=jnp.f...  14.2 us
    all_to_all x1, waiting for transfers between devices, body(): lax.all_to_all(mixed, 'seq', split_axis=0, concat_axis=0, tiled=True)  11.9 us
    unnamed x23, local copies, waits for them, and re-layouts  10.3 us
    ppermute x3, starting transfers between devices, shifted(): return lax.ppermute(value, axis, pairs)  10 us
  transfers between devices with their start and end apart: 6, of which 4 were waited for; matrix products, arithmetic and copies ran while one was open for 2% of the time, Pallas kernels for 0%

commit v1 on v0

--- a/solution.py
+++ b/solution.py
@@ -4,8 +4,15 @@
 import jax.numpy as jnp
 from jax import lax
 from jax.sharding import PartitionSpec as P
+from jax.lax import all_to_all, axis_size
 
 TRANSFORM_PRECISION = lax.Precision.HIGH
+
+
+def treat_array(panel, in_dim):
+    return jnp.concatenate(
+        all_to_all(jnp.stack([panel for _ in range(axis_size("tp"))]), "tp", 0, 0), axis=in_dim
+    )
 
 
 def shifted(value, axis, by):
@@ -96,9 +103,7 @@
         jnp.bfloat16
     )
     weights = lax.all_gather(out_weight, "seq", axis=0, tiled=True)
-    total = jnp.dot(
-        lax.all_gather(inner, "tp", axis=1, tiled=True), weights, preferred_element_type=jnp.float32
-    )
+    total = jnp.dot(treat_array(inner, 1), weights, preferred_element_type=jnp.float32)
     return total.astype(jnp.bfloat16)
 
 

time: 304 us -> 209 us (0.69)
  waiting for transfers between devices: 181 us -> 31.6 us
  blocking collectives: 38.1 us -> 88.3 us
  starting transfers between devices: 25.6 us -> 29.6 us
    all_gather x1, waiting for transfers between devices: 117 us -> 0.01 us  [body(): weights = lax.all_gather(out_weight, 'seq', axis=0, tiled=True)]
    all_to_all x0 -> x1, blocking collectives: none -> 50.2 us  [treat_array(): all_to_all(jnp.stack([panel for _ in range(axis_size('tp'))]), 'tp', 0, 0)]
    all_gather x1 -> x0, waiting for transfers between devices: 47.1 us -> none  [body(): lax.all_gather(inner, 'tp', axis=1, tiled=True)]
    all_to_all x1, waiting for transfers between devices: 11.9 us -> 25.8 us  [body(): lax.all_to_all(mixed, 'seq', split_axis=0, concat_axis=0, tiled=True)]
    all_to_all x1, starting transfers between devices: 15.5 us -> 19.5 us  [body(): lax.all_to_all(mixed, 'seq', split_axis=0, concat_axis=0, tiled=True)]
  transfers between devices with their start and end apart: 6 -> 5, of which waited for: 4 -> 2; matrix products, arithmetic and copies ran while one was open for 2% -> 17% of each run, Pallas kernels for 0% -> 0%
where the time goes in v1:
time: 209 us; the launch traced here: 207 us
  blocking collectives  88.3 us (42%)
  waiting for transfers between devices  31.6 us (15%)
  starting transfers between devices  29.6 us (14%)
  matrix products  20.7 us (10%)
  local copies, waits for them, and re-layouts  16.5 us (8%)
  between operations  13.7 us (7%)
  other arithmetic  6.28 us (3%)
    all_to_all x1, blocking collectives, treat_array(): all_to_all(jnp.stack([panel for _ in range(axis_size('tp'))]), 'tp', 0, 0)  50.2 us
    all_to_all x1, blocking collectives, body(): lax.all_to_all(outgoing, 'seq', split_axis=0, concat_axis=0, tiled=True)  38.1 us
    all_to_all x1, waiting for transfers between devices, body(): lax.all_to_all(mixed, 'seq', split_axis=0, concat_axis=0, tiled=True)  25.8 us
    all_to_all x1, starting transfers between devices, body(): lax.all_to_all(mixed, 'seq', split_axis=0, concat_axis=0, tiled=True)  19.5 us
    dot_general x4, matrix products, dot(): jnp.dot(a, b, precision=TRANSFORM_PRECISION, preferred_element_type=jnp.f...  14.2 us
    unnamed x23, local copies, waits for them, and re-layouts  10.3 us
    ppermute x3, starting transfers between devices, shifted(): return lax.ppermute(value, axis, pairs)  10 us
    dot_general x1, matrix products, body(): jnp.dot(treat_array(inner, 1), weights, preferred_element_type=jnp.float32)  6.53 us
  transfers between devices with their start and end apart: 5, of which 2 were waited for; matrix products, arithmetic and copies ran while one was open for 17% of the time, Pallas kernels for 0%

profile of v1, /device:TPU:1, one launch (start us, length us, event | category | flops | bytes accessed | tf_op | source)
XLA Modules:
  0.0 206.7 jit_solution(13400174672225979225)
XLA Ops:
  8.2 4.6 %collective-permute-start.1 = (bf16[2,1024]{0,1:T(8,128)(2,1)S(1)}, bf16[2,1024]{0,1:T(8,128)(2,1)S(1)}, u32[]{:S(2)}, u32[]{:S(2)}) collective-permute-start(bf16[2,1024]{0,1:T(8,128)(2,1)S(1)} %copy.23), channel_id=1, source_target_pairs={{0,4},{4,8},{8,12},{12,16},{16,20},{20,24},{24,28},{28,32},{32,36}... | collective-permute-start | bytes 12296 | tf_op jit(solution)/shard_map/ppermute | solution.py:21
  13.7 1.9 collective-permute-start.2
  15.6 0.9 fusion.19
  16.6 1.2 copy.22
  17.8 1.2 copy.25
  19.1 1.2 copy.28
  20.4 1.9 multiply_convert_fusion
  22.4 38.1 %all_to_all.15 = bf16[64,32,256]{2,1,0:T(8,128)(2,1)S(1)} all-to-all(bf16[64,32,256]{2,1,0:T(8,128)(2,1)S(1)} %pad_maximum_fusion.1), channel_id=1, replica_groups=mesh['seq'=64,'tp'=4] {'seq'}, dimensions={0} | all-to-all | bytes 2097152 | tf_op jit(solution)/shard_map/all_to_all | solution.py:98
  61.1 2.3 %fusion.20 = f32[256,8192]{1,0:T(8,128)S(1)} fusion(f32[256,64]{1,0:T(8,128)S(1)} %copy-done.5, bf16[64,8192]{1,0:T(8,128)(2,1)S(1)} %bitcast.73), kind=kOutput, calls=%fused_computation.43 | convolution fusion | flops 805306368 | bytes 9502720 | tf_op jit(solution)/shard_map/dot_general | solution.py:49
  64.4 1.2 fusion.4
  65.7 7.0 %fusion = f32[128,32,512]{2,0,1:T(8,128)S(1)} fusion(f32[512,512,1]{1,0,2:T(8,128)S(1)} %copy-done.1, f32[128,32,256]{2,0,1:T(8,128)S(1)} %get-tuple-element.6, f32[128,32,256]{2,0,1:T(8,128)S(1)} %get-tuple-element.5), kind=kOutput, calls=%fused_computation | convolution fusion | flops 6444548096 | bytes 17825792 | tf_op jit(solution)/shard_map/dot_general | solution.py:49
  72.7 0.8 multiply_subtract_fusion
  74.0 3.5 %fusion.6 = f32[128,16,512]{2,0,1:T(8,128)S(1)} fusion(f32[512,512,1]{1,0,2:T(8,128)S(1)} %copy-done, f32[128,16,256]{2,0,1:T(8,128)S(1)} %get-tuple-element.8, f32[128,16,256]{2,0,1:T(8,128)S(1)} %get-tuple-element.7), kind=kOutput, calls=%fused_computation.11 | convolution fusion | flops 3222274048 | bytes 9437184 | tf_op jit(solution)/shard_map/dot_general | solution.py:49
  78.5 2.4 %copy.33 = f32[2,128,16,256]{3,2,1,0:T(8,128)S(1)} copy(f32[2,128,16,256]{3,1,2,0:T(8,128)S(1)} %pad_maximum_fusion) | data formatting | bytes 8388608 | tf_op jit(solution)/shard_map/stack | solution.py:71
  80.9 3.8 %copy.37 = f32[32,8,16,256]{3,1,2,0:T(8,128)S(1)} copy(f32[32,8,16,256]{3,2,1,0:T(8,128)S(1)} %bitcast.68) | data formatting | bytes 8388608
  84.7 1.3 convolution_convert_fusion
  86.1 1.2 copy.38
  87.2 19.5 %all-to-all-start.1 = ((bf16[64,16,256]{2,1,0:T(8,128)(2,1)}), bf16[64,16,256]{2,1,0:T(8,128)(2,1)S(1)}, u32[]{:S(2)}, u32[]{:S(2)}) async-start(bf16[64,16,256]{2,1,0:T(8,128)(2,1)} %bitcast.36), calls=%async_computation.1 | async-start | bytes 1048576 | tf_op jit(solution)/shard_map/all_to_all | solution.py:100
  107.0 3.5 %collective-permute-start = (bf16[2,1024]{0,1:T(8,128)(2,1)S(1)}, bf16[2,1024]{0,1:T(8,128)(2,1)S(1)}, u32[]{:S(2)}, u32[]{:S(2)}) collective-permute-start(bf16[2,1024]{0,1:T(8,128)(2,1)S(1)} %copy.20), channel_id=1, source_target_pairs={{0,4},{4,8},{8,12},{12,16},{16,20},{20,24},{24,28},{28,32},{32,36}... | collective-permute-start | bytes 12296 | tf_op jit(solution)/shard_map/ppermute | solution.py:21
  110.8 5.0 %collective-permute-done = bf16[2,1024]{0,1:T(8,128)(2,1)S(1)} collective-permute-done((bf16[2,1024]{0,1:T(8,128)(2,1)S(1)}, bf16[2,1024]{0,1:T(8,128)(2,1)S(1)}, u32[]{:S(2)}, u32[]{:S(2)}) %collective-permute-start) | collective-permute-done | bytes 4128 | tf_op jit(solution)/shard_map/ppermute | solution.py:21
  115.8 25.8 %all-to-all-done.1 = bf16[64,16,256]{2,1,0:T(8,128)(2,1)S(1)} async-done(((bf16[64,16,256]{2,1,0:T(8,128)(2,1)}), bf16[64,16,256]{2,1,0:T(8,128)(2,1)S(1)}, u32[]{:S(2)}, u32[]{:S(2)}) %all-to-all-start.1) | async-done | bytes 524320 | tf_op jit(solution)/shard_map/all_to_all | solution.py:100
  141.7 1.3 fusion.12
  143.1 50.2 %all_to_all.16 = bf16[4,256,1024]{1,2,0:T(8,128)(2,1)S(1)} all-to-all(bf16[4,256,1024]{1,2,0:T(8,128)(2,1)S(1)} %stack.19), channel_id=1, replica_groups=mesh['seq'=64,'tp'=4] {'tp'}, dimensions={0} | all-to-all | bytes 4194304 | tf_op jit(solution)/shard_map/all_to_all | solution.py:14
  193.3 6.5 %convolution_convert_fusion.1 = bf16[256,1024]{1,0:T(8,128)(2,1)} fusion(bf16[256,4096]{0,1:T(8,128)(2,1)S(1)} %bitcast.71, bf16[4096,1024]{1,0:T(8,128)(2,1)} %all-gather.2.cloned.1.call-done), kind=kOutput, calls=%fused_computation.20 | convolution fusion | flops 2147745792 | bytes 11010048 | tf_op jit(solution)/shard_map/dot_general | solution.py:106
  (34 shorter events, 6.3 us)
Async XLA Ops:
  6.5 186.7 %all-gather.2.cloned.1.call-start = ((), (), s32[]{:S(2)}) async-start(), calls=%async_computation.3 | async-start | bytes 8519680 | tf_op jit(solution)/shard_map/all_gather | solution.py:105
  8.2 12.1 %collective-permute-start.1 = (bf16[2,1024]{0,1:T(8,128)(2,1)S(1)}, bf16[2,1024]{0,1:T(8,128)(2,1)S(1)}, u32[]{:S(2)}, u32[]{:S(2)}) collective-permute-start(bf16[2,1024]{0,1:T(8,128)(2,1)S(1)} %copy.23), channel_id=1, source_target_pairs={{0,4},{4,8},{8,12},{12,16},{16,20},{20,24},{24,28},{28,32},{32,36}... | collective-permute-start | bytes 12296 | tf_op jit(solution)/shard_map/ppermute | solution.py:21
  13.7 6.6 %collective-permute-start.2 = (bf16[2,1024]{0,1:T(8,128)(2,1)S(1)}, bf16[2,1024]{0,1:T(8,128)(2,1)S(1)}, u32[]{:S(2)}, u32[]{:S(2)}) collective-permute-start(bf16[2,1024]{0,1:T(8,128)(2,1)S(1)} %copy.26), channel_id=1, source_target_pairs={{0,4},{4,8},{8,12},{12,16},{16,20},{20,24},{24,28},{28,32},{32,36}... | collective-permute-start | bytes 12296 | tf_op jit(solution)/shard_map/ppermute | solution.py:21
  20.3 40.8 %copy-start.5 = (f32[256,64]{1,0:T(8,128)S(1)}, f32[256,64]{1,0:T(8,128)}, u32[]{:S(2)}) copy-start(f32[256,64]{1,0:T(8,128)} %constant.12.clone) | copy-start | bytes 196612
  63.4 0.9 copy-start.3
  63.4 1.0 copy-start.4
  64.4 1.3 copy-start.1
  72.7 1.2 copy-start
  80.9 3.8 %copy-start.6 = (f32[64,256]{1,0:T(8,128)S(1)}, f32[64,256]{1,0:T(8,128)}, u32[]{:S(2)}) copy-start(f32[64,256]{1,0:T(8,128)} %constant.17.clone) | copy-start | bytes 196612
  84.7 22.1 %copy-start.2 = (bf16[256,1024]{1,0:T(8,128)(2,1)S(1)}, bf16[256,1024]{1,0:T(8,128)(2,1)}, u32[]{:S(2)}) copy-start(bf16[256,1024]{1,0:T(8,128)(2,1)} %param.13) | copy-start | bytes 1572868
  84.7 56.9 %copy-start.7 = (f32[1024]{0:T(1024)S(1)}, f32[1024]{0:T(1024)}, u32[]{:S(2)}) copy-start(f32[1024]{0:T(1024)} %param.18) | copy-start | bytes 12292
  87.2 54.4 %all-to-all-start.1 = ((bf16[64,16,256]{2,1,0:T(8,128)(2,1)}), bf16[64,16,256]{2,1,0:T(8,128)(2,1)S(1)}, u32[]{:S(2)}, u32[]{:S(2)}) async-start(bf16[64,16,256]{2,1,0:T(8,128)(2,1)} %bitcast.36), calls=%async_computation.1 | async-start | bytes 1048576 | tf_op jit(solution)/shard_map/all_to_all | solution.py:100
  107.0 8.8 %collective-permute-start = (bf16[2,1024]{0,1:T(8,128)(2,1)S(1)}, bf16[2,1024]{0,1:T(8,128)(2,1)S(1)}, u32[]{:S(2)}, u32[]{:S(2)}) collective-permute-start(bf16[2,1024]{0,1:T(8,128)(2,1)S(1)} %copy.20), channel_id=1, source_target_pairs={{0,4},{4,8},{8,12},{12,16},{16,20},{20,24},{24,28},{28,32},{32,36}... | collective-permute-start | bytes 12296 | tf_op jit(solution)/shard_map/ppermute | solution.py:21
Sparse Core Ops, SparseCore 0:
  10.9 141.8 all-gather.1
